TPU v7x, 512 devices: a whole 4x8x8 slice. The times are simulated.
512 devices in a mesh: head: 16 (over y, core), seq: 32 (over z, x).
Axes of the slice: x: 4, y: 8, z: 8, core: 2. Of those that a mesh axis runs over, the one named last changes fastest.
Arguments:
- queries: bfloat16 [32768, 2048], P(('seq', 'head'))
- keys: bfloat16 [32768, 2048], P(('seq', 'head'))
- values: bfloat16 [32768, 2048], P(('seq', 'head')), may hold values from -6 to 6
- grad_out: bfloat16 [32768, 2048], P(('seq', 'head')), may hold values from -6 to 6
- random_blocks: int32 [256, 3], P('seq'), may hold values from 0 to 255, as said below
Outputs:
- attended: bfloat16 [32768, 2048], P(('seq', 'head'))
- grad_queries: bfloat16 [32768, 2048], P(('seq', 'head'))
- grad_keys: bfloat16 [32768, 2048], P(('seq', 'head'))
- grad_values: bfloat16 [32768, 2048], P(('seq', 'head'))
Inputs may be any that keep to these rules, and one draw needn't show every extreme that they name: `random_blocks`: within the rows of one sequence group (8 consecutive query blocks), at most 2 entries name blocks of any one group's range of 8 blocks, and in every group's rows one group's range is named exactly 2 times.
All inputs are finite; a program needn't handle non-finite values.
Results may differ from a plain program's by a relative error of at most 0.022.
Values may be sent and summed in bfloat16 or wider, within the bound.
No kernel may reach another device: no remote copies, remote signals or barrier semaphores. Data moves between devices by JAX's collectives and lax.ppermute only.
A program may use at most 192 MiB of HBM per device.

v0:
```python
import jax
import jax.numpy as jnp
from jax import lax
from jax.sharding import PartitionSpec as P

HD = 128
BLK = 128
RAND = 3


def with_halo(cells, sides, width):
    for axis, dim in sides:
        count = lax.axis_size(axis)
        ends = count - 1
        head = lax.slice_in_dim(cells, 0, width, axis=dim)
        tail = lax.slice_in_dim(cells, cells.shape[dim] - width, cells.shape[dim], axis=dim)
        cells = jnp.concatenate(
            [
                lax.ppermute(tail, axis, [(i, (i + 1) % count) for i in range(ends)]),
                cells,
                lax.ppermute(head, axis, [((i + 1) % count, i) for i in range(ends)]),
            ],
            axis=dim,
        )
    return cells


def broadcast(value, axis, source):
    kept = jnp.where(lax.axis_index(axis) == source, value, 0).astype(value.dtype)
    return lax.psum(kept, axis)


def slot_places(owners, groups, capacity):
    owner_hits = (owners[:, None] == jnp.arange(groups, dtype=jnp.int32)[None, :]).astype(jnp.int32)
    earlier = jnp.cumsum(owner_hits, axis=0) - owner_hits
    return owners * capacity + jnp.sum(earlier * owner_hits, axis=1)


def request_table(list_rows, query_count, groups, capacity):
    flat_rows = list_rows.reshape(-1)
    places = slot_places(flat_rows // query_count, groups, capacity)
    matches = places[None, :] == jnp.arange(groups * capacity, dtype=jnp.int32)[:, None]
    table = jnp.sum(jnp.where(matches, (flat_rows % query_count)[None, :], 0), axis=1)
    return table.reshape(groups, capacity)


def window_valid(my_group, query_count, groups):
    block_ids = jnp.arange(query_count, dtype=jnp.int32)
    left_ok = jnp.logical_not(jnp.logical_and(my_group == 0, block_ids == 0))
    right_ok = jnp.logical_not(
        jnp.logical_and(my_group == groups - 1, block_ids == query_count - 1)
    )
    all_true = jnp.ones((query_count, BLK), dtype=bool)
    return jnp.concatenate(
        [
            all_true,
            all_true,
            left_ok[:, None] & all_true,
            all_true,
            right_ok[:, None] & all_true,
            jnp.ones((query_count, RAND * BLK), dtype=bool),
        ],
        axis=1,
    )


def against_keys(rows, global_part, window_part, remote_part):
    return jnp.concatenate(
        [
            jnp.einsum("qihd,jhd->qhij", rows, global_part, preferred_element_type=jnp.float32),
            jnp.einsum("qihd,qjhd->qhij", rows, window_part, preferred_element_type=jnp.float32),
            jnp.einsum("qihd,qjhd->qhij", rows, remote_part, preferred_element_type=jnp.float32),
        ],
        axis=-1,
    )


def split_keys(table):
    return (table[..., : 2 * BLK], table[..., 2 * BLK : 5 * BLK], table[..., 5 * BLK :])


def weigh_keys(table, global_part, window_part, remote_part):
    global_w, window_w, random_w = split_keys(table)
    return (
        jnp.einsum("qhij,jhd->qihd", global_w, global_part, preferred_element_type=jnp.float32)
        + jnp.einsum("qhij,qjhd->qihd", window_w, window_part, preferred_element_type=jnp.float32)
        + jnp.einsum("qhij,qjhd->qihd", random_w, remote_part, preferred_element_type=jnp.float32)
    )


def key_terms(table, rows):
    global_w, window_w, random_w = split_keys(table)
    return (
        jnp.einsum("qhij,qihd->jhd", global_w, rows, preferred_element_type=jnp.float32),
        jnp.einsum("qhij,qihd->qjhd", window_w, rows, preferred_element_type=jnp.float32),
        jnp.einsum("qhij,qihd->qjhd", random_w, rows, preferred_element_type=jnp.float32),
    )


def shards(queries, keys, values, grad_out, random_blocks):
    groups = lax.axis_size("seq")
    my_group = lax.axis_index("seq")
    head_q, head_k, head_v, head_g = (
        lax.all_to_all(queries, "head", split_axis=1, concat_axis=0, tiled=True),
        lax.all_to_all(keys, "head", split_axis=1, concat_axis=0, tiled=True),
        lax.all_to_all(values, "head", split_axis=1, concat_axis=0, tiled=True),
        lax.all_to_all(grad_out, "head", split_axis=1, concat_axis=0, tiled=True),
    )
    group_tokens = head_q.shape[0]
    head_count = head_q.shape[1] // HD
    query_count = group_tokens // BLK
    capacity = max(2, 3 * query_count * RAND // (2 * groups))
    score_scale = HD ** (-0.5)
    key_value = jnp.stack([head_k, head_v])
    kv_blocks = key_value.reshape(2, query_count, BLK, head_count, HD)
    edged = with_halo(key_value, (("seq", 1),), BLK)
    edged = edged.reshape(2, query_count + 2, BLK, head_count, HD)
    window_kv = jnp.concatenate(
        [edged[:, 0:query_count], edged[:, 1 : query_count + 1], edged[:, 2 : query_count + 2]],
        axis=2,
    )
    global_kv = broadcast(kv_blocks[:, 0:2].reshape(2, 2 * BLK, head_count, HD), "seq", 0)
    flat_ids = random_blocks.reshape(-1)
    places = slot_places(flat_ids // query_count, groups, capacity)
    wanted = lax.all_to_all(
        request_table(random_blocks, query_count, groups, capacity),
        "seq",
        split_axis=0,
        concat_axis=0,
        tiled=True,
    )
    served = jnp.take(kv_blocks, wanted.reshape(-1), axis=1)
    served = served.reshape(2, groups, capacity, BLK, head_count, HD)
    fetched = lax.all_to_all(served, "seq", split_axis=1, concat_axis=1, tiled=True)
    chosen = jnp.take(fetched.reshape(2, groups * capacity, BLK, head_count, HD), places, axis=1)
    remote_kv = chosen.reshape(2, query_count, RAND * BLK, head_count, HD)
    query_blocks = head_q.reshape(query_count, BLK, head_count, HD)
    grad_blocks = head_g.reshape(query_count, BLK, head_count, HD)
    scores = score_scale * against_keys(query_blocks, global_kv[0], window_kv[0], remote_kv[0])
    valid = window_valid(my_group, query_count, groups)
    scores = jnp.where(valid[:, None, None, :], scores, -jnp.inf)
    row_max = jnp.max(scores, axis=-1, keepdims=True)
    exponent = jnp.exp(scores - row_max)
    attention_probs = exponent / jnp.sum(exponent, axis=-1, keepdims=True)
    weights = attention_probs.astype(jnp.bfloat16)
    attended = weigh_keys(weights, global_kv[1], window_kv[1], remote_kv[1]).astype(jnp.bfloat16)
    grad_prob = against_keys(grad_blocks, global_kv[1], window_kv[1], remote_kv[1])
    row_delta = jnp.sum(attention_probs * grad_prob, axis=-1, keepdims=True)
    grad_score = (score_scale * attention_probs * (grad_prob - row_delta)).astype(jnp.bfloat16)
    grad_q = weigh_keys(grad_score, global_kv[0], window_kv[0], remote_kv[0]).astype(jnp.bfloat16)
    key_global, key_window, key_random = key_terms(grad_score, query_blocks)
    value_global, value_window, value_random = key_terms(weights, grad_blocks)
    global_sum = lax.psum(jnp.stack([key_global, value_global]).astype(jnp.bfloat16), "seq").astype(
        jnp.float32
    )
    window_grad = jnp.stack([key_window, value_window]).reshape(
        2, query_count, 3, BLK, head_count, HD
    )
    no_pad = (0, 0)
    extended = (
        jnp.pad(window_grad[:, :, 0], (no_pad, (0, 2), no_pad, no_pad, no_pad))
        + jnp.pad(window_grad[:, :, 1], (no_pad, (1, 1), no_pad, no_pad, no_pad))
        + jnp.pad(window_grad[:, :, 2], (no_pad, (2, 0), no_pad, no_pad, no_pad))
    )
    outward = jnp.concatenate([extended[:, 0], extended[:, query_count + 1]], axis=1)
    inward = with_halo(outward.astype(jnp.bfloat16), (("seq", 1),), BLK).astype(outward.dtype)
    own_grad = extended[:, 1 : query_count + 1]
    own_grad = own_grad.at[:, 0].add(inward[:, :BLK])
    own_grad = own_grad.at[:, query_count - 1].add(inward[:, 3 * BLK :])
    random_terms = (
        jnp.stack([key_random, value_random])
        .reshape(2, query_count * RAND, BLK, head_count, HD)
        .astype(jnp.bfloat16)
    )
    send_pick = (places[None, :] == jnp.arange(groups * capacity, dtype=jnp.int32)[:, None]).astype(
        jnp.bfloat16
    )
    outgoing = jnp.einsum(
        "pj,xjihd->xpihd", send_pick, random_terms, preferred_element_type=jnp.float32
    ).astype(jnp.bfloat16)
    incoming = lax.all_to_all(
        outgoing.reshape(2, groups, capacity, BLK, head_count, HD),
        "seq",
        split_axis=1,
        concat_axis=1,
        tiled=True,
    )
    take_pick = (
        wanted.reshape(-1)[None, :] == jnp.arange(query_count, dtype=jnp.int32)[:, None]
    ).astype(jnp.bfloat16)
    random_sum = jnp.einsum(
        "qp,xpihd->xqihd",
        take_pick,
        incoming.reshape(2, groups * capacity, BLK, head_count, HD),
        preferred_element_type=jnp.float32,
    )
    global_sum = global_sum.reshape(2, 2, BLK, head_count, HD)
    own_grad = own_grad.at[:, 0:2].add(jnp.where(my_group == 0, global_sum, 0.0))
    total_grad = own_grad + random_sum
    grad_k = total_grad[0].reshape(group_tokens, head_count * HD).astype(jnp.bfloat16)
    grad_v = total_grad[1].reshape(group_tokens, head_count * HD).astype(jnp.bfloat16)
    return (
        lax.all_to_all(
            attended.reshape(group_tokens, head_count * HD),
            "head",
            split_axis=0,
            concat_axis=1,
            tiled=True,
        ),
        lax.all_to_all(
            grad_q.reshape(group_tokens, head_count * HD),
            "head",
            split_axis=0,
            concat_axis=1,
            tiled=True,
        ),
        lax.all_to_all(grad_k, "head", split_axis=0, concat_axis=1, tiled=True),
        lax.all_to_all(grad_v, "head", split_axis=0, concat_axis=1, tiled=True),
    )


def solution(mesh):
    placed = (
        P(("seq", "head"), None),
        P(("seq", "head"), None),
        P(("seq", "head"), None),
        P(("seq", "head"), None),
        P("seq", None),
    )
    return jax.shard_map(
        shards,
        mesh=mesh,
        in_specs=placed,
        out_specs=(
            P(("seq", "head"), None),
            P(("seq", "head"), None),
            P(("seq", "head"), None),
            P(("seq", "head"), None),
        ),
        check_vma=False,
    )
```

profile of v0, /device:TPU:1, one launch (start us, length us, event | category | flops | bytes accessed | tf_op | source)
XLA Modules:
  0.0 558.6 jit_solution(16468300619809350168)
XLA Ops:
  9.3 13.7 %all-to-all-start.3 = ((s32[32,1,2]{2,1,0:T(1,128)}), s32[32,1,2]{2,1,0:T(1,128)S(1)}, u32[]{:S(2)}, u32[]{:S(2)}) async-start(s32[32,1,2]{2,1,0:T(1,128)} %bitcast.20), calls=%async_computation.3 | async-start | bytes 32768 | tf_op jit(solution)/shard_map/all_to_all | solution.py:125
  23.8 7.7 %all-to-all-done.3 = s32[32,1,2]{2,1,0:T(1,128)S(1)} async-done(((s32[32,1,2]{2,1,0:T(1,128)}), s32[32,1,2]{2,1,0:T(1,128)S(1)}, u32[]{:S(2)}, u32[]{:S(2)}) %all-to-all-start.3) | async-done | bytes 288 | tf_op jit(solution)/shard_map/all_to_all | solution.py:125
  31.5 9.2 %all-to-all-start.2 = ((bf16[64,16,128]{2,0,1:T(8,128)(2,1)}), bf16[64,16,128]{2,0,1:T(8,128)(2,1)S(1)}, u32[]{:S(2)}, u32[]{:S(2)}) async-start(bf16[64,16,128]{2,0,1:T(8,128)(2,1)} %copy_bitcast_fusion.8), calls=%async_computation.2 | async-start | bytes 524288 | tf_op jit(solution)/shard_map/all_to_all | solution.py:104
  40.7 1.7 copy_bitcast_fusion.10
  42.4 10.0 %all-to-all-done.2 = bf16[64,16,128]{2,0,1:T(8,128)(2,1)S(1)} async-done(((bf16[64,16,128]{2,0,1:T(8,128)(2,1)}), bf16[64,16,128]{2,0,1:T(8,128)(2,1)S(1)}, u32[]{:S(2)}, u32[]{:S(2)}) %all-to-all-start.2) | async-done | bytes 262176 | tf_op jit(solution)/shard_map/all_to_all | solution.py:104
  52.4 3.4 all-to-all-start
  58.8 8.2 %all-to-all-done = bf16[64,16,128]{2,0,1:T(8,128)(2,1)S(1)} async-done(((bf16[64,16,128]{2,0,1:T(8,128)(2,1)}), bf16[64,16,128]{2,0,1:T(8,128)(2,1)S(1)}, u32[]{:S(2)}, u32[]{:S(2)}) %all-to-all-start) | async-done | bytes 262176 | tf_op jit(solution)/shard_map/all_to_all | solution.py:105
  67.0 3.4 all-to-all-start.1
  70.6 11.6 %all-to-all-done.1 = bf16[64,16,128]{2,0,1:T(8,128)(2,1)S(1)} async-done(((bf16[64,16,128]{2,0,1:T(8,128)(2,1)}), bf16[64,16,128]{2,0,1:T(8,128)(2,1)S(1)}, u32[]{:S(2)}, u32[]{:S(2)}) %all-to-all-start.1) | async-done | bytes 262176 | tf_op jit(solution)/shard_map/all_to_all | solution.py:106
  82.1 3.4 all-to-all-start.6
  85.6 3.0 gather_fusion
  88.7 2.7 copy.169
  91.9 2.5 copy.170
  94.4 2.3 all-to-all-done.6
  96.7 4.9 all-to-all-start.4
  101.9 3.0 collective-permute-start
  104.9 1.5 collective-permute-start.1
  107.0 7.4 %collective-permute-done = bf16[2,128,128]{2,1,0:T(8,128)(2,1)S(1)} collective-permute-done((bf16[2,128,128]{2,1,0:T(8,128)(2,1)S(1)}, bf16[2,128,128]{2,1,0:T(8,128)(2,1)S(1)}, u32[]{:S(2)}, u32[]{:S(2)}) %collective-permute-start) | collective-permute-done | bytes 65568 | tf_op jit(solution)/shard_map/ppermute | solution.py:19
  116.2 1.5 convolution_bitcast_fusion.1
  117.7 159.4 %all-reduce.6.cloned.1.call-done = bf16[2,256,1,128]{3,1,2,0:T(8,128)(2,1)} async-done(((bf16[2,256,1,128]{3,1,2,0:T(8,128)(2,1)}), bf16[2,256,1,128]{3,1,2,0:T(8,128)(2,1)}) %all-reduce.6.cloned.1.call-update) | async-done | bytes 131088 | tf_op jit(solution)/shard_map/psum | solution.py:30
  278.2 2.1 convolution_bitcast_fusion.5
  280.4 4.8 copy.171
  285.2 4.1 gather_fusion.1
  289.3 1.6 bitcast_select_fusion
  291.5 1.4 fusion.20
  292.9 1.5 fusion.2
  296.1 1.9 multiply_reduce_fusion
  298.0 2.3 multiply_convert_fusion
  302.9 1.4 convolution_convert_fusion
  304.3 6.7 %copy.190 = bf16[2,32,2,128,1,128]{5,2,3,0,4,1:T(2,128)(2,1)} copy(bf16[2,32,2,128,1,128]{5,2,1,3,0,4:T(2,128)(2,1)S(1)} %bitcast.319) | data formatting | bytes 8388608 | tf_op jit(solution)/shard_map/reshape | solution.py:182
  311.0 6.0 %all-to-all-start.8 = ((bf16[2,32,2,128,1,128]{5,2,3,0,4,1:T(2,128)(2,1)}), bf16[2,32,2,128,1,128]{5,2,3,0,4,1:T(2,128)(2,1)}, u32[]{:S(2)}, u32[]{:S(2)}) async-start(bf16[2,32,2,128,1,128]{5,2,3,0,4,1:T(2,128)(2,1)} %copy.190), calls=%async_computation.8 | async-start | bytes 8388608 | tf_op jit(solution)/shard_map/all_to_all | solution.py:181
  317.4 1.3 fusion.17
  319.7 1.5 fusion.22
  322.4 3.3 collective-permute-start.2
  325.8 1.4 collective-permute-start.3
  331.7 4.2 collective-permute-done.3
  336.7 3.0 scatter-add.11
  339.7 68.0 %all-to-all-done.8 = bf16[2,32,2,128,1,128]{5,2,3,0,4,1:T(2,128)(2,1)} async-done(((bf16[2,32,2,128,1,128]{5,2,3,0,4,1:T(2,128)(2,1)}), bf16[2,32,2,128,1,128]{5,2,3,0,4,1:T(2,128)(2,1)}, u32[]{:S(2)}, u32[]{:S(2)}) %all-to-all-start.8) | async-done | bytes 4194336 | tf_op jit(solution)/shard_map/all_to_all | solution.py:181
  407.7 14.6 %all-to-all-start.7 = ((bf16[16,64,128]{2,1,0:T(8,128)(2,1)}), bf16[16,64,128]{2,1,0:T(8,128)(2,1)S(1)}, u32[]{:S(2)}, u32[]{:S(2)}) async-start(bf16[16,64,128]{2,1,0:T(8,128)(2,1)} %bitcast.67), calls=%async_computation.7 | async-start | bytes 524288 | tf_op jit(solution)/shard_map/all_to_all | solution.py:210
  422.3 65.6 %all-reduce.8.cloned.1.call-done = bf16[2,256,1,128]{3,1,2,0:T(8,128)(2,1)} async-done(((bf16[2,256,1,128]{3,1,2,0:T(8,128)(2,1)}), bf16[2,256,1,128]{3,1,2,0:T(8,128)(2,1)}) %all-reduce.8.cloned.1.call-update) | async-done | bytes 131088 | tf_op jit(solution)/shard_map/psum | solution.py:153
  489.1 9.0 %copy.191 = bf16[2,32,2,128,1,128]{5,2,1,3,0,4:T(2,128)(2,1)} copy(bf16[2,32,2,128,1,128]{5,2,3,0,4,1:T(2,128)(2,1)} %all-to-all-done.8) | data formatting | bytes 8388608 | tf_op jit(solution)/shard_map/all_to_all | solution.py:181
  498.1 11.5 %all-to-all-start.5 = ((bf16[16,64,128]{2,1,0:T(8,128)(2,1)}), bf16[16,64,128]{2,1,0:T(8,128)(2,1)S(1)}, u32[]{:S(2)}, u32[]{:S(2)}) async-start(bf16[16,64,128]{2,1,0:T(8,128)(2,1)} %bitcast.45), calls=%async_computation.5 | async-start | bytes 524288 | tf_op jit(solution)/shard_map/all_to_all | solution.py:203
  509.7 2.8 fusion.7
  513.3 8.1 %all-to-all-done.5 = bf16[16,64,128]{2,1,0:T(8,128)(2,1)S(1)} async-done(((bf16[16,64,128]{2,1,0:T(8,128)(2,1)}), bf16[16,64,128]{2,1,0:T(8,128)(2,1)S(1)}, u32[]{:S(2)}, u32[]{:S(2)}) %all-to-all-start.5) | async-done | bytes 262176 | tf_op jit(solution)/shard_map/all_to_all | solution.py:203
  521.4 3.4 all-to-all-start.10
  526.3 9.6 %all-to-all-done.10 = bf16[16,64,128]{2,1,0:T(8,128)(2,1)S(1)} async-done(((bf16[16,64,128]{2,1,0:T(8,128)(2,1)}), bf16[16,64,128]{2,1,0:T(8,128)(2,1)S(1)}, u32[]{:S(2)}, u32[]{:S(2)}) %all-to-all-start.10) | async-done | bytes 262176 | tf_op jit(solution)/shard_map/all_to_all | solution.py:218
  535.9 3.4 all-to-all-start.9
  540.8 10.2 %all-to-all-done.9 = bf16[16,64,128]{2,1,0:T(8,128)(2,1)S(1)} async-done(((bf16[16,64,128]{2,1,0:T(8,128)(2,1)}), bf16[16,64,128]{2,1,0:T(8,128)(2,1)S(1)}, u32[]{:S(2)}, u32[]{:S(2)}) %all-to-all-start.9) | async-done | bytes 262176 | tf_op jit(solution)/shard_map/all_to_all | solution.py:217
  (124 shorter events, 28.3 us)
Async XLA Ops:
  7.2 15.8 %copy-start = (bf16[64,2048]{1,0:T(8,128)(2,1)S(1)}, bf16[64,2048]{1,0:T(8,128)(2,1)}, u32[]{:S(2)}) copy-start(bf16[64,2048]{1,0:T(8,128)(2,1)} %param.11) | copy-start | bytes 786436
  7.2 48.7 %copy-start.17 = (bf16[64,2048]{1,0:T(8,128)(2,1)S(1)}, bf16[64,2048]{1,0:T(8,128)(2,1)}, u32[]{:S(2)}) copy-start(bf16[64,2048]{1,0:T(8,128)(2,1)} %param.13) | copy-start | bytes 786436
  7.2 49.4 %copy-start.18 = (bf16[64,2048]{1,0:T(8,128)(2,1)S(1)}, bf16[64,2048]{1,0:T(8,128)(2,1)}, u32[]{:S(2)}) copy-start(bf16[64,2048]{1,0:T(8,128)(2,1)} %param.14) | copy-start | bytes 786436
  9.3 22.2 %all-to-all-start.3 = ((s32[32,1,2]{2,1,0:T(1,128)}), s32[32,1,2]{2,1,0:T(1,128)S(1)}, u32[]{:S(2)}, u32[]{:S(2)}) async-start(s32[32,1,2]{2,1,0:T(1,128)} %bitcast.20), calls=%async_computation.3 | async-start | bytes 32768 | tf_op jit(solution)/shard_map/all_to_all | solution.py:125
  31.5 20.9 %all-to-all-start.2 = ((bf16[64,16,128]{2,0,1:T(8,128)(2,1)}), bf16[64,16,128]{2,0,1:T(8,128)(2,1)S(1)}, u32[]{:S(2)}, u32[]{:S(2)}) async-start(bf16[64,16,128]{2,0,1:T(8,128)(2,1)} %copy_bitcast_fusion.8), calls=%async_computation.2 | async-start | bytes 524288 | tf_op jit(solution)/shard_map/all_to_all | solution.py:104
  52.4 14.6 %all-to-all-start = ((bf16[64,16,128]{2,0,1:T(8,128)(2,1)}), bf16[64,16,128]{2,0,1:T(8,128)(2,1)S(1)}, u32[]{:S(2)}, u32[]{:S(2)}) async-start(bf16[64,16,128]{2,0,1:T(8,128)(2,1)} %copy_bitcast_fusion.10), calls=%async_computation | async-start | bytes 524288 | tf_op jit(solution)/shard_map/all_to_all | solution.py:105
  67.0 15.1 %all-to-all-start.1 = ((bf16[64,16,128]{2,0,1:T(8,128)(2,1)}), bf16[64,16,128]{2,0,1:T(8,128)(2,1)S(1)}, u32[]{:S(2)}, u32[]{:S(2)}) async-start(bf16[64,16,128]{2,0,1:T(8,128)(2,1)} %copy_bitcast_fusion.9), calls=%async_computation.1 | async-start | bytes 524288 | tf_op jit(solution)/shard_map/all_to_all | solution.py:106
  82.1 14.5 %all-to-all-start.6 = ((bf16[64,16,128]{2,0,1:T(8,128)(2,1)}), bf16[64,16,128]{2,0,1:T(8,128)(2,1)S(1)}, u32[]{:S(2)}, u32[]{:S(2)}) async-start(bf16[64,16,128]{2,0,1:T(8,128)(2,1)} %copy_bitcast_fusion.7), calls=%async_computation.6 | async-start | bytes 524288 | tf_op jit(solution)/shard_map/all_to_all | solution.py:107
  96.7 183.7 %all-to-all-start.4 = ((bf16[2,32,2,128,1,128]{5,3,2,0,4,1:T(8,128)(2,1)}), bf16[2,32,2,128,1,128]{5,3,2,0,4,1:T(8,128)(2,1)}, u32[]{:S(2)}, u32[]{:S(2)}) async-start(bf16[2,32,2,128,1,128]{5,3,2,0,4,1:T(8,128)(2,1)} %copy.170), calls=%async_computation.4 | async-start | bytes 8388608 | tf_op jit(solution)/shard_map/all_to_all | solution.py:134
  101.5 175.6 %all-reduce.6.cloned.1.call-start = ((), (), s32[]{:S(2)}) async-start(), calls=%async_computation.11 | async-start | bytes 262144 | tf_op jit(solution)/shard_map/psum | solution.py:30
  101.9 12.5 %collective-permute-start = (bf16[2,128,128]{2,1,0:T(8,128)(2,1)S(1)}, bf16[2,128,128]{2,1,0:T(8,128)(2,1)S(1)}, u32[]{:S(2)}, u32[]{:S(2)}) collective-permute-start(bf16[2,128,128]{2,1,0:T(8,128)(2,1)S(1)} %get-tuple-element.58), channel_id=1, source_target_pairs={{0,1},{1,2},{2,3},{3,4},{4,5},{5,6},{6,7},{7,8},{8,9},{9,10},{10,1... | collective-permute-start | bytes 196616 | tf_op jit(solution)/shard_map/ppermute | solution.py:19
  104.9 9.6 %collective-permute-start.1 = (bf16[2,128,128]{2,1,0:T(8,128)(2,1)S(1)}, bf16[2,128,128]{2,1,0:T(8,128)(2,1)S(1)}, u32[]{:S(2)}, u32[]{:S(2)}) collective-permute-start(bf16[2,128,128]{2,1,0:T(8,128)(2,1)S(1)} %get-tuple-element.59), channel_id=1, source_target_pairs={{1,0},{2,1},{3,2},{4,3},{5,4},{6,5},{7,6},{8,7},{9,8},{10,9},{11,1... | collective-permute-start | bytes 196616 | tf_op jit(solution)/shard_map/ppermute | solution.py:21
  115.0 1.1 copy-start.6
  291.1 1.8 copy-start.10
  291.1 3.3 copy-start.12
  294.4 1.4 copy-start.8
  294.4 1.7 copy-start.9
  300.4 1.4 copy-start.2
  300.4 2.0 copy-start.4
  311.0 7.8 %copy-start.3 = (bf16[8,1,128,1024]{2,3,0,1:T(8,128)(2,1)S(1)}, bf16[8,1,128,1024]{2,3,0,1:T(8,128)(2,1)}, u32[]{:S(2)}) copy-start(bf16[8,1,128,1024]{2,3,0,1:T(8,128)(2,1)} %copy-done.2) | copy-start | bytes 6291460
  311.0 96.8 %all-to-all-start.8 = ((bf16[2,32,2,128,1,128]{5,2,3,0,4,1:T(2,128)(2,1)}), bf16[2,32,2,128,1,128]{5,2,3,0,4,1:T(2,128)(2,1)}, u32[]{:S(2)}, u32[]{:S(2)}) async-start(bf16[2,32,2,128,1,128]{5,2,3,0,4,1:T(2,128)(2,1)} %copy.190), calls=%async_computation.8 | async-start | bytes 8388608 | tf_op jit(solution)/shard_map/all_to_all | solution.py:181
  317.0 170.9 %all-reduce.8.cloned.1.call-start = ((), (), s32[]{:S(2)}) async-start(), calls=%async_computation.12 | async-start | bytes 262144 | tf_op jit(solution)/shard_map/psum | solution.py:153
  322.1 5.1 copy-start.16
  322.4 5.6 copy-start.14
  322.4 4.9 copy-start.5
  322.4 5.6 copy-start.13
  322.4 9.2 %collective-permute-start.2 = (bf16[2,128,1,128]{3,1,0,2:T(8,128)(2,1)S(1)}, bf16[2,128,1,128]{3,1,0,2:T(8,128)(2,1)S(1)}, u32[]{:S(2)}, u32[]{:S(2)}) collective-permute-start(bf16[2,128,1,128]{3,1,0,2:T(8,128)(2,1)S(1)} %get-tuple-element.49), channel_id=1, source_target_pairs={{0,1},{1,2},{2,3},{3,4},{4,5},{5,6},{6,7},{7,8},{8,9},{9,10},{10,1... | collective-permute-start | bytes 196616 | tf_op jit(solution)/shard_map/ppermute | solution.py:19
  325.8 2.6 copy-start.11
  325.8 10.1 %collective-permute-start.3 = (bf16[2,128,1,128]{3,1,0,2:T(8,128)(2,1)S(1)}, bf16[2,128,1,128]{3,1,0,2:T(8,128)(2,1)S(1)}, u32[]{:S(2)}, u32[]{:S(2)}) collective-permute-start(bf16[2,128,1,128]{3,1,0,2:T(8,128)(2,1)S(1)} %get-tuple-element.50), channel_id=1, source_target_pairs={{1,0},{2,1},{3,2},{4,3},{5,4},{6,5},{7,6},{8,7},{9,8},{10,9},{11,1... | collective-permute-start | bytes 196616 | tf_op jit(solution)/shard_map/ppermute | solution.py:21
  327.9 1.4 copy-start.7
  330.5 5.4 copy-start.15
  330.5 5.4 slice-start
  407.7 90.4 %all-to-all-start.7 = ((bf16[16,64,128]{2,1,0:T(8,128)(2,1)}), bf16[16,64,128]{2,1,0:T(8,128)(2,1)S(1)}, u32[]{:S(2)}, u32[]{:S(2)}) async-start(bf16[16,64,128]{2,1,0:T(8,128)(2,1)} %bitcast.67), calls=%async_computation.7 | async-start | bytes 524288 | tf_op jit(solution)/shard_map/all_to_all | solution.py:210
  498.1 23.2 %all-to-all-start.5 = ((bf16[16,64,128]{2,1,0:T(8,128)(2,1)}), bf16[16,64,128]{2,1,0:T(8,128)(2,1)S(1)}, u32[]{:S(2)}, u32[]{:S(2)}) async-start(bf16[16,64,128]{2,1,0:T(8,128)(2,1)} %bitcast.45), calls=%async_computation.5 | async-start | bytes 524288 | tf_op jit(solution)/shard_map/all_to_all | solution.py:203
  512.5 39.3 %copy-start.1 = (bf16[64,2048]{1,0:T(8,128)(2,1)S(1)}, bf16[64,2048]{1,0:T(8,128)(2,1)}, u32[]{:S(2)}) copy-start(bf16[64,2048]{1,0:T(8,128)(2,1)} %param.11) | copy-start | bytes 786436
  521.4 14.6 %all-to-all-start.10 = ((bf16[16,64,128]{2,1,0:T(8,128)(2,1)}), bf16[16,64,128]{2,1,0:T(8,128)(2,1)S(1)}, u32[]{:S(2)}, u32[]{:S(2)}) async-start(bf16[16,64,128]{2,1,0:T(8,128)(2,1)} %bitcast.126), calls=%async_computation.10 | async-start | bytes 524288 | tf_op jit(solution)/shard_map/all_to_all | solution.py:218
  535.9 15.1 %all-to-all-start.9 = ((bf16[16,64,128]{2,1,0:T(8,128)(2,1)}), bf16[16,64,128]{2,1,0:T(8,128)(2,1)S(1)}, u32[]{:S(2)}, u32[]{:S(2)}) async-start(bf16[16,64,128]{2,1,0:T(8,128)(2,1)} %bitcast.124), calls=%async_computation.9 | async-start | bytes 524288 | tf_op jit(solution)/shard_map/all_to_all | solution.py:217
Sparse Core Ops, SparseCore 0:
  107.2 169.8 all-reduce.5
  322.3 165.5 all-reduce.7
where the time goes:
time: 560 us; the launch traced here: 559 us
  waiting for transfers between devices  372 us (66%)
  starting transfers between devices  86.6 us (15%)
  local copies, waits for them, and re-layouts  53 us (9%)
  matrix products  18.1 us (3%)
  between operations  14.7 us (3%)
  other arithmetic  13.9 us (2%)
    psum x1, waiting for transfers between devices, broadcast(): return lax.psum(kept, axis)  159 us
    all_to_all x1, waiting for transfers between devices, shards(): lax.all_to_all(outgoing.reshape(2, groups, capacity, BLK, head_count, HD)...  68 us
    psum x1, waiting for transfers between devices, shards(): lax.psum(jnp.stack([key_global, value_global]).astype(jnp.bfloat16), 'seq')  65.6 us
    all_to_all x1, starting transfers between devices, shards(): lax.all_to_all(grad_q.reshape(group_tokens, head_count * HD), 'head', spl...  14.6 us
    all_to_all x1, starting transfers between devices, shards(): lax.all_to_all(request_table(random_blocks, query_count, groups, capacity...  13.7 us
    all_to_all x1, waiting for transfers between devices, shards(): lax.all_to_all(values, 'head', split_axis=1, concat_axis=0, tiled=True)  11.6 us
    all_to_all x1, starting transfers between devices, shards(): lax.all_to_all(attended.reshape(group_tokens, head_count * HD), 'head', s...  11.5 us
  transfers between devices with their start and end apart: 17, of which 13 were waited for; matrix products, arithmetic and copies ran while one was open for 9% of the time, Pallas kernels for 0%

commit v1 on v0

--- a/solution.py
+++ b/solution.py
@@ -6,6 +6,12 @@
 HD = 128
 BLK = 128
 RAND = 3
+
+
+def measure_types_on_mesh(mat, axis_id):
+    g_now = lax.all_gather(mat, axis_name=axis_id)
+    r_now = jnp.sum(g_now, 0)
+    return r_now
 
 
 def with_halo(cells, sides, width):
@@ -150,9 +156,9 @@
     grad_q = weigh_keys(grad_score, global_kv[0], window_kv[0], remote_kv[0]).astype(jnp.bfloat16)
     key_global, key_window, key_random = key_terms(grad_score, query_blocks)
     value_global, value_window, value_random = key_terms(weights, grad_blocks)
-    global_sum = lax.psum(jnp.stack([key_global, value_global]).astype(jnp.bfloat16), "seq").astype(
-        jnp.float32
-    )
+    global_sum = measure_types_on_mesh(
+        jnp.stack([key_global, value_global]).astype(jnp.bfloat16), "seq"
+    ).astype(jnp.float32)
     window_grad = jnp.stack([key_window, value_window]).reshape(
         2, query_count, 3, BLK, head_count, HD
     )

time: 560 us -> 506 us (0.904)
  waiting for transfers between devices: 372 us -> 309 us
  starting transfers between devices: 86.6 us -> 93.5 us
    psum x1 -> x0, waiting for transfers between devices: 65.6 us -> none  [shards(): lax.psum(jnp.stack([key_global, value_global]).astype(jnp.bfloat16), 'seq')]
    all_to_all x1, starting transfers between devices: 14.6 us -> 25.9 us  [shards(): lax.all_to_all(grad_q.reshape(group_tokens, head_count * HD), 'head', spl...]
  transfers between devices with their start and end apart: 17 -> 17, of which waited for: 13 -> 12; matrix products, arithmetic and copies ran while one was open for 9% -> 10% of each run, Pallas kernels for 0% -> 0%
where the time goes in v1:
time: 506 us; the launch traced here: 503 us
  waiting for transfers between devices  309 us (61%)
  starting transfers between devices  93.5 us (18%)
  local copies, waits for them, and re-layouts  52.9 us (10%)
  matrix products  17.1 us (3%)
  other arithmetic  15.8 us (3%)
  between operations  14.8 us (3%)
    psum x1, waiting for transfers between devices, broadcast(): return lax.psum(kept, axis)  159 us
    all_to_all x1, waiting for transfers between devices, shards(): lax.all_to_all(outgoing.reshape(2, groups, capacity, BLK, head_count, HD)...  69.6 us
    all_to_all x1, starting transfers between devices, shards(): lax.all_to_all(grad_q.reshape(group_tokens, head_count * HD), 'head', spl...  25.9 us
    all_to_all x1, starting transfers between devices, shards(): lax.all_to_all(request_table(random_blocks, query_count, groups, capacity...  13.7 us
    all_to_all x1, waiting for transfers between devices, shards(): lax.all_to_all(values, 'head', split_axis=1, concat_axis=0, tiled=True)  11.6 us
    all_to_all x1, waiting for transfers between devices, shards(): lax.all_to_all(grad_k, 'head', split_axis=0, concat_axis=1, tiled=True)  10.2 us
  transfers between devices with their start and end apart: 17, of which 12 were waited for; matrix products, arithmetic and copies ran while one was open for 10% of the time, Pallas kernels for 0%

profile of v1, /device:TPU:1, one launch (start us, length us, event | category | flops | bytes accessed | tf_op | source)
XLA Modules:
  0.0 503.0 jit_solution(3612377534694347022)
XLA Ops:
  9.3 13.7 %all-to-all-start.3 = ((s32[32,1,2]{2,1,0:T(1,128)}), s32[32,1,2]{2,1,0:T(1,128)S(1)}, u32[]{:S(2)}, u32[]{:S(2)}) async-start(s32[32,1,2]{2,1,0:T(1,128)} %bitcast.20), calls=%async_computation.3 | async-start | bytes 32768 | tf_op jit(solution)/shard_map/all_to_all | solution.py:131
  23.8 7.7 %all-to-all-done.3 = s32[32,1,2]{2,1,0:T(1,128)S(1)} async-done(((s32[32,1,2]{2,1,0:T(1,128)}), s32[32,1,2]{2,1,0:T(1,128)S(1)}, u32[]{:S(2)}, u32[]{:S(2)}) %all-to-all-start.3) | async-done | bytes 288 | tf_op jit(solution)/shard_map/all_to_all | solution.py:131
  31.5 9.2 %all-to-all-start.2 = ((bf16[64,16,128]{2,0,1:T(8,128)(2,1)}), bf16[64,16,128]{2,0,1:T(8,128)(2,1)S(1)}, u32[]{:S(2)}, u32[]{:S(2)}) async-start(bf16[64,16,128]{2,0,1:T(8,128)(2,1)} %copy_bitcast_fusion.8), calls=%async_computation.2 | async-start | bytes 524288 | tf_op jit(solution)/shard_map/all_to_all | solution.py:110
  40.7 1.7 copy_bitcast_fusion.10
  42.4 10.0 %all-to-all-done.2 = bf16[64,16,128]{2,0,1:T(8,128)(2,1)S(1)} async-done(((bf16[64,16,128]{2,0,1:T(8,128)(2,1)}), bf16[64,16,128]{2,0,1:T(8,128)(2,1)S(1)}, u32[]{:S(2)}, u32[]{:S(2)}) %all-to-all-start.2) | async-done | bytes 262176 | tf_op jit(solution)/shard_map/all_to_all | solution.py:110
  52.4 3.4 all-to-all-start
  58.8 8.2 %all-to-all-done = bf16[64,16,128]{2,0,1:T(8,128)(2,1)S(1)} async-done(((bf16[64,16,128]{2,0,1:T(8,128)(2,1)}), bf16[64,16,128]{2,0,1:T(8,128)(2,1)S(1)}, u32[]{:S(2)}, u32[]{:S(2)}) %all-to-all-start) | async-done | bytes 262176 | tf_op jit(solution)/shard_map/all_to_all | solution.py:111
  67.0 3.4 all-to-all-start.1
  70.6 11.6 %all-to-all-done.1 = bf16[64,16,128]{2,0,1:T(8,128)(2,1)S(1)} async-done(((bf16[64,16,128]{2,0,1:T(8,128)(2,1)}), bf16[64,16,128]{2,0,1:T(8,128)(2,1)S(1)}, u32[]{:S(2)}, u32[]{:S(2)}) %all-to-all-start.1) | async-done | bytes 262176 | tf_op jit(solution)/shard_map/all_to_all | solution.py:112
  82.1 3.4 all-to-all-start.6
  85.6 3.0 gather_fusion
  88.7 2.7 copy.168
  91.9 2.5 copy.169
  94.4 2.3 all-to-all-done.6
  96.7 4.9 all-to-all-start.4
  101.9 3.0 collective-permute-start
  104.9 1.5 collective-permute-start.1
  107.0 7.4 %collective-permute-done = bf16[2,128,128]{2,1,0:T(8,128)(2,1)S(1)} collective-permute-done((bf16[2,128,128]{2,1,0:T(8,128)(2,1)S(1)}, bf16[2,128,128]{2,1,0:T(8,128)(2,1)S(1)}, u32[]{:S(2)}, u32[]{:S(2)}) %collective-permute-start) | collective-permute-done | bytes 65568 | tf_op jit(solution)/shard_map/ppermute | solution.py:25
  116.2 1.5 convolution_bitcast_fusion.1
  117.7 159.4 %all-reduce.5.cloned.1.call-done = bf16[2,256,1,128]{3,1,2,0:T(8,128)(2,1)} async-done(((bf16[2,256,1,128]{3,1,2,0:T(8,128)(2,1)}), bf16[2,256,1,128]{3,1,2,0:T(8,128)(2,1)}) %all-reduce.5.cloned.1.call-update) | async-done | bytes 131088 | tf_op jit(solution)/shard_map/psum | solution.py:36
  278.2 2.1 convolution_bitcast_fusion.5
  280.4 4.8 copy.170
  285.2 4.2 gather_fusion.1
  289.3 1.6 bitcast_select_fusion
  291.5 1.4 fusion.20
  292.9 1.5 fusion.2
  296.1 1.9 multiply_reduce_fusion
  298.0 2.3 multiply_convert_fusion
  303.4 1.4 convolution_convert_fusion
  304.7 6.7 %copy.189 = bf16[2,32,2,128,1,128]{5,2,3,0,4,1:T(2,128)(2,1)} copy(bf16[2,32,2,128,1,128]{5,2,1,3,0,4:T(2,128)(2,1)S(1)} %bitcast.319) | data formatting | bytes 8388608 | tf_op jit(solution)/shard_map/reshape | solution.py:188
  311.4 5.9 %all-to-all-start.8 = ((bf16[2,32,2,128,1,128]{5,2,3,0,4,1:T(2,128)(2,1)}), bf16[2,32,2,128,1,128]{5,2,3,0,4,1:T(2,128)(2,1)}, u32[]{:S(2)}, u32[]{:S(2)}) async-start(bf16[2,32,2,128,1,128]{5,2,3,0,4,1:T(2,128)(2,1)} %copy.189), calls=%async_computation.8 | async-start | bytes 8388608 | tf_op jit(solution)/shard_map/all_to_all | solution.py:187
  318.4 1.5 fusion.22
  321.1 3.3 collective-permute-start.2
  324.5 1.4 collective-permute-start.3
  329.2 1.1 fusion.13
  330.4 4.9 collective-permute-done.3
  336.1 3.0 scatter-add.11
  339.0 69.6 %all-to-all-done.8 = bf16[2,32,2,128,1,128]{5,2,3,0,4,1:T(2,128)(2,1)} async-done(((bf16[2,32,2,128,1,128]{5,2,3,0,4,1:T(2,128)(2,1)}), bf16[2,32,2,128,1,128]{5,2,3,0,4,1:T(2,128)(2,1)}, u32[]{:S(2)}, u32[]{:S(2)}) %all-to-all-start.8) | async-done | bytes 4194336 | tf_op jit(solution)/shard_map/all_to_all | solution.py:187
  408.6 25.9 %all-to-all-start.7 = ((bf16[16,64,128]{2,1,0:T(8,128)(2,1)}), bf16[16,64,128]{2,1,0:T(8,128)(2,1)S(1)}, u32[]{:S(2)}, u32[]{:S(2)}) async-start(bf16[16,64,128]{2,1,0:T(8,128)(2,1)} %bitcast.67), calls=%async_computation.7 | async-start | bytes 524288 | tf_op jit(solution)/shard_map/all_to_all | solution.py:216
  434.5 9.0 %copy.190 = bf16[2,32,2,128,1,128]{5,2,1,3,0,4:T(2,128)(2,1)} copy(bf16[2,32,2,128,1,128]{5,2,3,0,4,1:T(2,128)(2,1)} %all-to-all-done.8) | data formatting | bytes 8388608 | tf_op jit(solution)/shard_map/all_to_all | solution.py:187
  443.6 2.8 reduce_sum.59
  446.7 7.2 %all-to-all-start.5 = ((bf16[16,64,128]{2,1,0:T(8,128)(2,1)}), bf16[16,64,128]{2,1,0:T(8,128)(2,1)S(1)}, u32[]{:S(2)}, u32[]{:S(2)}) async-start(bf16[16,64,128]{2,1,0:T(8,128)(2,1)} %bitcast.45), calls=%async_computation.5 | async-start | bytes 524288 | tf_op jit(solution)/shard_map/all_to_all | solution.py:209
  454.0 2.8 fusion.7
  457.6 8.1 %all-to-all-done.5 = bf16[16,64,128]{2,1,0:T(8,128)(2,1)S(1)} async-done(((bf16[16,64,128]{2,1,0:T(8,128)(2,1)}), bf16[16,64,128]{2,1,0:T(8,128)(2,1)S(1)}, u32[]{:S(2)}, u32[]{:S(2)}) %all-to-all-start.5) | async-done | bytes 262176 | tf_op jit(solution)/shard_map/all_to_all | solution.py:209
  465.7 3.4 all-to-all-start.10
  470.6 9.6 %all-to-all-done.10 = bf16[16,64,128]{2,1,0:T(8,128)(2,1)S(1)} async-done(((bf16[16,64,128]{2,1,0:T(8,128)(2,1)}), bf16[16,64,128]{2,1,0:T(8,128)(2,1)S(1)}, u32[]{:S(2)}, u32[]{:S(2)}) %all-to-all-start.10) | async-done | bytes 262176 | tf_op jit(solution)/shard_map/all_to_all | solution.py:224
  480.2 3.4 all-to-all-start.9
  485.2 10.2 %all-to-all-done.9 = bf16[16,64,128]{2,1,0:T(8,128)(2,1)S(1)} async-done(((bf16[16,64,128]{2,1,0:T(8,128)(2,1)}), bf16[16,64,128]{2,1,0:T(8,128)(2,1)S(1)}, u32[]{:S(2)}, u32[]{:S(2)}) %all-to-all-start.9) | async-done | bytes 262176 | tf_op jit(solution)/shard_map/all_to_all | solution.py:223
  (125 shorter events, 26.5 us)
Async XLA Ops:
  7.2 15.8 %copy-start = (bf16[64,2048]{1,0:T(8,128)(2,1)S(1)}, bf16[64,2048]{1,0:T(8,128)(2,1)}, u32[]{:S(2)}) copy-start(bf16[64,2048]{1,0:T(8,128)(2,1)} %param.11) | copy-start | bytes 786436
  7.2 48.7 %copy-start.17 = (bf16[64,2048]{1,0:T(8,128)(2,1)S(1)}, bf16[64,2048]{1,0:T(8,128)(2,1)}, u32[]{:S(2)}) copy-start(bf16[64,2048]{1,0:T(8,128)(2,1)} %param.13) | copy-start | bytes 786436
  7.2 49.4 %copy-start.18 = (bf16[64,2048]{1,0:T(8,128)(2,1)S(1)}, bf16[64,2048]{1,0:T(8,128)(2,1)}, u32[]{:S(2)}) copy-start(bf16[64,2048]{1,0:T(8,128)(2,1)} %param.14) | copy-start | bytes 786436
  9.3 22.2 %all-to-all-start.3 = ((s32[32,1,2]{2,1,0:T(1,128)}), s32[32,1,2]{2,1,0:T(1,128)S(1)}, u32[]{:S(2)}, u32[]{:S(2)}) async-start(s32[32,1,2]{2,1,0:T(1,128)} %bitcast.20), calls=%async_computation.3 | async-start | bytes 32768 | tf_op jit(solution)/shard_map/all_to_all | solution.py:131
  31.5 20.9 %all-to-all-start.2 = ((bf16[64,16,128]{2,0,1:T(8,128)(2,1)}), bf16[64,16,128]{2,0,1:T(8,128)(2,1)S(1)}, u32[]{:S(2)}, u32[]{:S(2)}) async-start(bf16[64,16,128]{2,0,1:T(8,128)(2,1)} %copy_bitcast_fusion.8), calls=%async_computation.2 | async-start | bytes 524288 | tf_op jit(solution)/shard_map/all_to_all | solution.py:110
  52.4 14.6 %all-to-all-start = ((bf16[64,16,128]{2,0,1:T(8,128)(2,1)}), bf16[64,16,128]{2,0,1:T(8,128)(2,1)S(1)}, u32[]{:S(2)}, u32[]{:S(2)}) async-start(bf16[64,16,128]{2,0,1:T(8,128)(2,1)} %copy_bitcast_fusion.10), calls=%async_computation | async-start | bytes 524288 | tf_op jit(solution)/shard_map/all_to_all | solution.py:111
  67.0 15.1 %all-to-all-start.1 = ((bf16[64,16,128]{2,0,1:T(8,128)(2,1)}), bf16[64,16,128]{2,0,1:T(8,128)(2,1)S(1)}, u32[]{:S(2)}, u32[]{:S(2)}) async-start(bf16[64,16,128]{2,0,1:T(8,128)(2,1)} %copy_bitcast_fusion.9), calls=%async_computation.1 | async-start | bytes 524288 | tf_op jit(solution)/shard_map/all_to_all | solution.py:112
  82.1 14.5 %all-to-all-start.6 = ((bf16[64,16,128]{2,0,1:T(8,128)(2,1)}), bf16[64,16,128]{2,0,1:T(8,128)(2,1)S(1)}, u32[]{:S(2)}, u32[]{:S(2)}) async-start(bf16[64,16,128]{2,0,1:T(8,128)(2,1)} %copy_bitcast_fusion.7), calls=%async_computation.6 | async-start | bytes 524288 | tf_op jit(solution)/shard_map/all_to_all | solution.py:113
  96.7 183.7 %all-to-all-start.4 = ((bf16[2,32,2,128,1,128]{5,3,2,0,4,1:T(8,128)(2,1)}), bf16[2,32,2,128,1,128]{5,3,2,0,4,1:T(8,128)(2,1)}, u32[]{:S(2)}, u32[]{:S(2)}) async-start(bf16[2,32,2,128,1,128]{5,3,2,0,4,1:T(8,128)(2,1)} %copy.169), calls=%async_computation.4 | async-start | bytes 8388608 | tf_op jit(solution)/shard_map/all_to_all | solution.py:140
  101.5 175.6 %all-reduce.5.cloned.1.call-start = ((), (), s32[]{:S(2)}) async-start(), calls=%async_computation.11 | async-start | bytes 262144 | tf_op jit(solution)/shard_map/psum | solution.py:36
  101.9 12.5 %collective-permute-start = (bf16[2,128,128]{2,1,0:T(8,128)(2,1)S(1)}, bf16[2,128,128]{2,1,0:T(8,128)(2,1)S(1)}, u32[]{:S(2)}, u32[]{:S(2)}) collective-permute-start(bf16[2,128,128]{2,1,0:T(8,128)(2,1)S(1)} %get-tuple-element.58), channel_id=1, source_target_pairs={{0,1},{1,2},{2,3},{3,4},{4,5},{5,6},{6,7},{7,8},{8,9},{9,10},{10,1... | collective-permute-start | bytes 196616 | tf_op jit(solution)/shard_map/ppermute | solution.py:25
  104.9 9.6 %collective-permute-start.1 = (bf16[2,128,128]{2,1,0:T(8,128)(2,1)S(1)}, bf16[2,128,128]{2,1,0:T(8,128)(2,1)S(1)}, u32[]{:S(2)}, u32[]{:S(2)}) collective-permute-start(bf16[2,128,128]{2,1,0:T(8,128)(2,1)S(1)} %get-tuple-element.59), channel_id=1, source_target_pairs={{1,0},{2,1},{3,2},{4,3},{5,4},{6,5},{7,6},{8,7},{9,8},{10,9},{11,1... | collective-permute-start | bytes 196616 | tf_op jit(solution)/shard_map/ppermute | solution.py:27
  115.0 1.2 copy-start.6
  291.1 1.8 copy-start.10
  291.1 3.3 copy-start.12
  294.4 1.4 copy-start.8
  294.4 1.7 copy-start.9
  300.4 1.4 copy-start.2
  300.4 2.0 copy-start.4
  311.4 97.3 %all-to-all-start.8 = ((bf16[2,32,2,128,1,128]{5,2,3,0,4,1:T(2,128)(2,1)}), bf16[2,32,2,128,1,128]{5,2,3,0,4,1:T(2,128)(2,1)}, u32[]{:S(2)}, u32[]{:S(2)}) async-start(bf16[2,32,2,128,1,128]{5,2,3,0,4,1:T(2,128)(2,1)} %copy.189), calls=%async_computation.8 | async-start | bytes 8388608 | tf_op jit(solution)/shard_map/all_to_all | solution.py:187
  317.3 2.6 copy-start.3
  317.3 126.2 %all-gather.2.cloned.1.call-start = ((), (), s32[]{:S(2)}) async-start(), calls=%async_computation.12 | async-start | bytes 4325376 | tf_op jit(solution)/shard_map/all_gather | solution.py:12
  320.8 5.1 %copy-start.16 = (bf16[2,256,1,128]{3,1,2,0:T(8,128)(2,1)S(1)}, bf16[2,256,1,128]{3,1,2,0:T(8,128)(2,1)}, u32[]{:S(2)}) copy-start(bf16[2,256,1,128]{3,1,2,0:T(8,128)(2,1)} %all-reduce.5.cloned.1.call-done) | copy-start | bytes 393220
  321.0 5.6 %copy-start.14 = (f32[2,10,128,1,128]{4,2,0,3,1:T(8,128)}, f32[2,10,128,1,128]{4,2,0,3,1:T(8,128)S(1)}, u32[]{:S(2)}) copy-start(f32[2,10,128,1,128]{4,2,0,3,1:T(8,128)S(1)} %bitcast_add_fusion) | copy-start | bytes 3932164
  321.1 4.9 copy-start.5
  321.1 5.6 %copy-start.13 = (bf16[1,24,128,1,128]{4,2,0,1,3:T(8,128)(2,1)S(1)}, bf16[1,24,128,1,128]{4,2,0,1,3:T(8,128)(2,1)}, u32[]{:S(2)}) copy-start(bf16[1,24,128,1,128]{4,2,0,1,3:T(8,128)(2,1)} %copy-done.12) | copy-start | bytes 2359300
  321.1 9.2 %collective-permute-start.2 = (bf16[2,128,1,128]{3,1,0,2:T(8,128)(2,1)S(1)}, bf16[2,128,1,128]{3,1,0,2:T(8,128)(2,1)S(1)}, u32[]{:S(2)}, u32[]{:S(2)}) collective-permute-start(bf16[2,128,1,128]{3,1,0,2:T(8,128)(2,1)S(1)} %get-tuple-element.49), channel_id=1, source_target_pairs={{0,1},{1,2},{2,3},{3,4},{4,5},{5,6},{6,7},{7,8},{8,9},{9,10},{10,1... | collective-permute-start | bytes 196616 | tf_op jit(solution)/shard_map/ppermute | solution.py:25
  324.5 2.6 copy-start.11
  324.5 10.8 %collective-permute-start.3 = (bf16[2,128,1,128]{3,1,0,2:T(8,128)(2,1)S(1)}, bf16[2,128,1,128]{3,1,0,2:T(8,128)(2,1)S(1)}, u32[]{:S(2)}, u32[]{:S(2)}) collective-permute-start(bf16[2,128,1,128]{3,1,0,2:T(8,128)(2,1)S(1)} %get-tuple-element.50), channel_id=1, source_target_pairs={{1,0},{2,1},{3,2},{4,3},{5,4},{6,5},{7,6},{8,7},{9,8},{10,9},{11,1... | collective-permute-start | bytes 196616 | tf_op jit(solution)/shard_map/ppermute | solution.py:27
  326.7 1.4 copy-start.7
  329.2 6.0 %copy-start.15 = (f32[2,10,128,1,128]{4,2,0,3,1:T(8,128)S(1)}, f32[2,10,128,1,128]{4,2,0,3,1:T(8,128)}, u32[]{:S(2)}) copy-start(f32[2,10,128,1,128]{4,2,0,3,1:T(8,128)} %copy-done.14) | copy-start | bytes 3932164
  329.2 6.0 %slice-start = ((f32[2,10,128,1,128]{4,2,0,3,1:T(8,128)}), f32[2,8,128,1,128]{4,2,0,3,1:T(8,128)S(1)}, s32[]{:S(2)}) async-start(f32[2,10,128,1,128]{4,2,0,3,1:T(8,128)} %copy-done.14), calls=%async_computation.13 | async-start | bytes 2097152 | tf_op jit(solution)/shard_map/slice | solution.py:173
  408.6 38.1 %all-to-all-start.7 = ((bf16[16,64,128]{2,1,0:T(8,128)(2,1)}), bf16[16,64,128]{2,1,0:T(8,128)(2,1)S(1)}, u32[]{:S(2)}, u32[]{:S(2)}) async-start(bf16[16,64,128]{2,1,0:T(8,128)(2,1)} %bitcast.67), calls=%async_computation.7 | async-start | bytes 524288 | tf_op jit(solution)/shard_map/all_to_all | solution.py:216
  446.7 18.9 %all-to-all-start.5 = ((bf16[16,64,128]{2,1,0:T(8,128)(2,1)}), bf16[16,64,128]{2,1,0:T(8,128)(2,1)S(1)}, u32[]{:S(2)}, u32[]{:S(2)}) async-start(bf16[16,64,128]{2,1,0:T(8,128)(2,1)} %bitcast.45), calls=%async_computation.5 | async-start | bytes 524288 | tf_op jit(solution)/shard_map/all_to_all | solution.py:209
  456.9 39.3 %copy-start.1 = (bf16[64,2048]{1,0:T(8,128)(2,1)S(1)}, bf16[64,2048]{1,0:T(8,128)(2,1)}, u32[]{:S(2)}) copy-start(bf16[64,2048]{1,0:T(8,128)(2,1)} %param.11) | copy-start | bytes 786436
  465.7 14.6 %all-to-all-start.10 = ((bf16[16,64,128]{2,1,0:T(8,128)(2,1)}), bf16[16,64,128]{2,1,0:T(8,128)(2,1)S(1)}, u32[]{:S(2)}, u32[]{:S(2)}) async-start(bf16[16,64,128]{2,1,0:T(8,128)(2,1)} %bitcast.126), calls=%async_computation.10 | async-start | bytes 524288 | tf_op jit(solution)/shard_map/all_to_all | solution.py:224
  480.2 15.1 %all-to-all-start.9 = ((bf16[16,64,128]{2,1,0:T(8,128)(2,1)}), bf16[16,64,128]{2,1,0:T(8,128)(2,1)S(1)}, u32[]{:S(2)}, u32[]{:S(2)}) async-start(bf16[16,64,128]{2,1,0:T(8,128)(2,1)} %bitcast.124), calls=%async_computation.9 | async-start | bytes 524288 | tf_op jit(solution)/shard_map/all_to_all | solution.py:223
Sparse Core Ops, SparseCore 0:
  107.2 169.8 all-reduce.4
  322.4 116.7 all-gather.1
